TPU v7x, 256 devices: a whole 4x4x8 slice. The times are simulated.
256 devices in a mesh: grp: 4 (over x), tok: 8 (over z), mdl: 8 (over y, core).
Axes of the slice: x: 4, y: 4, z: 8, core: 2. Of those that a mesh axis runs over, the one named last changes fastest.
Arguments:
- hidden_in: bfloat16 [4, 1024, 5120], P('grp', 'tok', 'mdl'), may hold values from -8 to 8
- seg_ids: int32 [4, 1024], replicated, may hold values from 0 to 3, never falling along the last dimension, each value on 1 to 768 neighbouring positions
- request_prefix: int32 [4, 4], replicated, may hold values from 0 to 1
- page_table: int32 [32], replicated, may hold values from 0 to 31, each once
- prefix_cache: bfloat16 [32, 256, 8, 256], P(('grp', 'mdl'), None, 'tok'), may hold values from -200 to 200
- attn_gain: float32 [5120], P('mdl'), may hold values from 0.1 to 1.9
- w_query: bfloat16 [5120, 5120], P('mdl', 'tok'), may hold values from -0.078125 to 0.078125
- w_key: bfloat16 [5120, 1024], P('mdl', 'tok'), may hold values from -0.25 to 0.25
- w_value: bfloat16 [5120, 1024], P('mdl', 'tok'), may hold values from -0.078125 to 0.078125
- w_out: bfloat16 [5120, 5120], P('tok', 'mdl'), may hold values from -0.078125 to 0.078125
- ffn_gain: float32 [5120], P('mdl'), may hold values from 0.1 to 1.9
- w_gate: bfloat16 [5120, 14336], P('mdl', 'tok'), may hold values from -0.078125 to 0.078125
- w_up: bfloat16 [5120, 14336], P('mdl', 'tok'), may hold values from -0.078125 to 0.078125
- w_down: bfloat16 [14336, 5120], P('tok', 'mdl'), may hold values from -0.046875 to 0.046875
- final_gain: float32 [5120], replicated, may hold values from 0.1 to 1.9
- lm_head: bfloat16 [76800, 5120], P(('grp', 'tok', 'mdl')), may hold values from -0.25 to 0.25
Outputs:
- hidden_out: bfloat16 [4, 1024, 5120], P('grp', 'tok', 'mdl')
- new_kv: bfloat16 [4, 1024, 8, 256], P('grp', 'mdl', 'tok')
- req_norm: float32 [4, 4], P('grp')
- max_logit: float32 [4, 4], replicated
- logits: float32 [16, 76800], P(None, ('grp', 'tok', 'mdl'))
Inputs may be any that keep to these rules, and one draw needn't show every extreme that they name: `seg_ids`: requests of a group are contiguous, in order, and none is empty. `page_table`: each physical slot holds exactly one logical page.
All inputs are finite; a program needn't handle non-finite values.
Results may differ from a plain program's by a relative error of at most 0.024.
Values may be sent and summed in bfloat16 or wider, within the bound.
No kernel may reach another device: no remote copies, remote signals or barrier semaphores. Data moves between devices by JAX's collectives and lax.ppermute only.
A program may use at most 128 MiB of HBM per device.

v0:
```python
import jax
import jax.numpy as jnp
from jax import lax
from jax.sharding import PartitionSpec as P

PREFIX = 4096
PAGE = 256
EPS = 1e-06
THETA = 1000000.0
NEG = -1e30


def rotate(tensor, positions):
    half_dim = tensor.shape[-1] // 2
    frequency = THETA ** (-(jnp.arange(half_dim, dtype=jnp.float32) * 2.0 / tensor.shape[-1]))
    angles = positions.astype(jnp.float32)[:, None] * frequency[None, :]
    cosine = jnp.cos(angles)[:, None, :]
    sine_part = jnp.sin(angles)[:, None, :]
    first_part = tensor[..., :half_dim]
    second = tensor[..., half_dim:]
    return jnp.concatenate(
        [first_part * cosine - second * sine_part, second * cosine + first_part * sine_part], -1
    )


def on_device(
    hidden_in,
    seg_ids,
    request_prefix,
    page_table,
    prefix_cache,
    attn_gain,
    w_query,
    w_key,
    w_value,
    w_out,
    ffn_gain,
    w_gate,
    w_up,
    w_down,
    final_gain,
    lm_head,
):
    groups_total = seg_ids.shape[0]
    seq_len = seg_ids.shape[1]
    req_count = request_prefix.shape[1]
    tok_rows = hidden_in.shape[1]
    feat_dev = hidden_in.shape[2]
    model_width = feat_dev * lax.axis_size("mdl")
    head_dim = prefix_cache.shape[3] // 2
    kv_dev = prefix_cache.shape[2]
    heads_dev = w_query.shape[1] // head_dim
    group_size = heads_dev // kv_dev
    page_len = prefix_cache.shape[1]
    slot_total = page_table.shape[0]
    rows_mdl = seq_len // lax.axis_size("mdl")
    group_idx = lax.axis_index("grp")
    tok_idx = lax.axis_index("tok")
    mdl_idx = lax.axis_index("mdl")
    score_scale = head_dim ** (-0.5)
    tokens = hidden_in[0].astype(jnp.float32)
    squares = lax.psum(jnp.sum(tokens * tokens, -1), "mdl")
    normed = (tokens * lax.rsqrt(squares[:, None] / model_width + EPS) * attn_gain).astype(
        jnp.bfloat16
    )
    w_joined = jnp.concatenate([w_query, w_key, w_value], 1)
    partial_qkv = jnp.dot(
        lax.all_gather(normed, "tok", axis=0, tiled=True),
        w_joined,
        preferred_element_type=jnp.float32,
    )
    qkv_rows = lax.psum_scatter(partial_qkv, "mdl", scatter_dimension=0, tiled=True)
    q_cols = heads_dev * head_dim
    kv_cols = kv_dev * head_dim
    queries = qkv_rows[:, :q_cols].reshape(rows_mdl, heads_dev, head_dim)
    key_rows = qkv_rows[:, q_cols : q_cols + kv_cols].reshape(rows_mdl, kv_dev, head_dim)
    value_rows = qkv_rows[:, q_cols + kv_cols :].reshape(rows_mdl, kv_dev, head_dim)
    seg_row = lax.dynamic_index_in_dim(seg_ids, group_idx, 0, keepdims=False)
    prefix_row = lax.dynamic_index_in_dim(request_prefix, group_idx, 0, keepdims=False)
    requests = jnp.arange(req_count, dtype=jnp.int32)
    member = seg_row[:, None] == requests[None, :]
    counts = jnp.sum(member.astype(jnp.int32), 0)
    offsets = jnp.cumsum(counts) - counts
    row_start = mdl_idx * rows_mdl
    my_rows = row_start + jnp.arange(rows_mdl, dtype=jnp.int32)
    my_seg = lax.dynamic_slice_in_dim(seg_row, row_start, rows_mdl)
    my_member = my_seg[:, None] == requests[None, :]
    positions = PREFIX + my_rows - jnp.sum(jnp.where(my_member, offsets[None, :], 0), 1)
    my_prefix = jnp.sum(jnp.where(my_member, prefix_row[None, :], 0), 1)
    q_rot = (
        rotate(queries, positions)
        .astype(jnp.bfloat16)
        .reshape(rows_mdl, kv_dev, group_size, head_dim)
    )
    k_rot = rotate(key_rows, positions).astype(jnp.bfloat16)
    appended = jnp.concatenate([k_rot, value_rows.astype(jnp.bfloat16)], -1)
    suffix = lax.all_gather(appended, "mdl", axis=0, tiled=True)
    every_row = jnp.arange(seq_len, dtype=jnp.int32)
    suffix_ok = ((seg_row[None, :] == my_seg[:, None]) & (every_row[None, :] <= my_rows[:, None]))[
        :, None, None, :
    ]
    suffix_scores = (
        jnp.einsum(
            "rcgd,tcd->rcgt", q_rot, suffix[..., :head_dim], preferred_element_type=jnp.float32
        )
        * score_scale
    )
    suffix_scores = jnp.where(suffix_ok, suffix_scores, NEG)
    row_max = jnp.max(suffix_scores, -1)
    suffix_weights = jnp.where(suffix_ok, jnp.exp(suffix_scores - row_max[..., None]), 0.0)
    row_total = jnp.sum(suffix_weights, -1)
    mixed = jnp.einsum(
        "rcgt,tcd->rcgd",
        suffix_weights.astype(jnp.bfloat16),
        suffix[..., head_dim:],
        preferred_element_type=jnp.float32,
    )
    slot_ids = jnp.arange(slot_total, dtype=jnp.int32)
    pages_each = PREFIX // PAGE
    slot_prefix = jnp.sum(
        jnp.where(page_table[None, :] == slot_ids[:, None], (slot_ids // pages_each)[None, :], 0), 1
    )
    piece = lax.all_gather(prefix_cache, ("grp", "mdl"), axis=0, tiled=True)
    page_count = piece.shape[0]
    key_prefix = jnp.repeat(slot_prefix, page_len)
    allowed = (my_prefix[:, None] == key_prefix[None, :])[:, None, None, :]
    flat_pages = piece.reshape(page_count * page_len, kv_dev, 2 * head_dim)
    scores = (
        jnp.einsum(
            "rcgd,kcd->rcgk", q_rot, flat_pages[..., :head_dim], preferred_element_type=jnp.float32
        )
        * score_scale
    )
    scores = jnp.where(allowed, scores, NEG)
    new_max = jnp.maximum(row_max, jnp.max(scores, -1))
    factor = jnp.exp(row_max - new_max)
    page_weights = jnp.where(allowed, jnp.exp(scores - new_max[..., None]), 0.0)
    new_total = row_total * factor + jnp.sum(page_weights, -1)
    new_mixed = mixed * factor[..., None] + jnp.einsum(
        "rcgk,kcd->rcgd",
        page_weights.astype(jnp.bfloat16),
        flat_pages[..., head_dim:],
        preferred_element_type=jnp.float32,
    )
    attended = (
        (new_mixed / new_total[..., None])
        .astype(jnp.bfloat16)
        .reshape(rows_mdl, heads_dev * head_dim)
    )
    partial_out = jnp.dot(
        lax.all_gather(attended, "mdl", axis=0, tiled=True),
        w_out,
        preferred_element_type=jnp.float32,
    )
    residual = tokens + lax.psum_scatter(
        partial_out.astype(jnp.bfloat16), "tok", scatter_dimension=0, tiled=True
    ).astype(jnp.float32)
    squares_ffn = lax.psum(jnp.sum(residual * residual, -1), "mdl")
    ffn_input = (residual * lax.rsqrt(squares_ffn[:, None] / model_width + EPS) * ffn_gain).astype(
        jnp.bfloat16
    )
    w_pair = jnp.concatenate([w_gate, w_up], 1)
    ff_dev = w_gate.shape[1]
    partial_ffn = jnp.dot(
        lax.all_gather(ffn_input, "tok", axis=0, tiled=True),
        w_pair,
        preferred_element_type=jnp.float32,
    )
    summed = lax.psum_scatter(
        partial_ffn.astype(jnp.bfloat16), "mdl", scatter_dimension=0, tiled=True
    ).astype(jnp.float32)
    activated = (jax.nn.silu(summed[:, :ff_dev]) * summed[:, ff_dev:]).astype(jnp.bfloat16)
    partial_down = jnp.dot(
        lax.all_gather(activated, "mdl", axis=0, tiled=True),
        w_down,
        preferred_element_type=jnp.float32,
    )
    final_rows = residual + lax.psum_scatter(
        partial_down.astype(jnp.bfloat16), "tok", scatter_dimension=0, tiled=True
    ).astype(jnp.float32)
    tok_start = tok_idx * tok_rows
    my_tok_rows = tok_start + jnp.arange(tok_rows, dtype=jnp.int32)
    tok_seg = lax.dynamic_slice_in_dim(seg_row, tok_start, tok_rows)
    row_squares = jnp.sum(final_rows * final_rows, -1)
    req_squares = jnp.sum(
        jnp.where(tok_seg[:, None] == requests[None, :], row_squares[:, None], 0.0), 0
    )
    ends = offsets + counts - 1
    picked = ends[:, None] == my_tok_rows[None, :]
    last_part = jnp.sum(jnp.where(picked[:, :, None], final_rows[None, :, :], 0.0), 1)
    padded = jnp.zeros((groups_total * req_count, model_width), jnp.float32)
    padded = lax.dynamic_update_slice(
        padded, last_part, (group_idx * req_count, mdl_idx * feat_dev)
    )
    req_total = lax.psum(req_squares, ("tok", "mdl"))
    last_all = lax.psum(padded, ("grp", "tok", "mdl"))
    req_norm = jnp.sqrt(req_total / (counts.astype(jnp.float32) * model_width) + EPS)
    last_normed = (
        last_all * lax.rsqrt(jnp.mean(last_all * last_all, -1, keepdims=True) + EPS) * final_gain
    ).astype(jnp.bfloat16)
    logits = lax.dot_general(
        last_normed, lm_head, (((1,), (1,)), ((), ())), preferred_element_type=jnp.float32
    )
    max_logit = lax.pmax(jnp.max(logits, -1), ("grp", "tok", "mdl")).reshape(
        groups_total, req_count
    )
    return (
        final_rows.astype(jnp.bfloat16)[None],
        appended[None],
        req_norm[None],
        max_logit,
        logits,
    )


def solution(mesh):
    return jax.shard_map(
        on_device,
        mesh=mesh,
        in_specs=(
            P("grp", "tok", "mdl"),
            P(),
            P(),
            P(),
            P(("grp", "mdl"), None, "tok", None),
            P("mdl"),
            P("mdl", "tok"),
            P("mdl", "tok"),
            P("mdl", "tok"),
            P("tok", "mdl"),
            P("mdl"),
            P("mdl", "tok"),
            P("mdl", "tok"),
            P("tok", "mdl"),
            P(),
            P(("grp", "tok", "mdl"), None),
        ),
        out_specs=(
            P("grp", "tok", "mdl"),
            P("grp", "mdl", "tok", None),
            P("grp", None),
            P(),
            P(None, ("grp", "tok", "mdl")),
        ),
        check_vma=False,
    )
```

profile of v0, /device:TPU:1, one launch (start us, length us, event | category | flops | bytes accessed | tf_op | source)
XLA Modules:
  0.0 899.1 jit_solution(10230812188905599163)
XLA Ops:
  9.2 15.0 %psum.28 = f32[128]{0:T(128)S(1)} all-reduce(f32[128]{0:T(128)S(1)} %fusion.44), channel_id=1, replica_groups=mesh['grp'=4,'tok'=8,'mdl'=8] {'mdl'}, use_global_device_ids=true, to_apply=%region_1.0 | all-reduce | flops 128 | bytes 1024 | tf_op jit(solution)/shard_map/psum | solution.py:62
  26.0 35.1 %all-gather.6.cloned.1.call-done = bf16[1024,640]{1,0:T(8,128)(2,1)} async-done(((bf16[128,640]{1,0:T(8,128)(2,1)}), bf16[1024,640]{1,0:T(8,128)(2,1)}) %all-gather.6.cloned.1.call-update) | async-done | bytes 1310736 | tf_op jit(solution)/shard_map/all_gather | solution.py:68
  61.1 5.1 fusion.30
  73.3 34.7 %reduce-scatter.5.cloned.1.call-done = f32[128,896]{0,1:T(8,128)} async-done(((f32[1024,896]{0,1:T(8,128)}), f32[128,896]{0,1:T(8,128)}) %reduce-scatter.5.cloned.1.call-update) | async-done | bytes 458768 | tf_op jit(solution)/shard_map/reduce_scatter | solution.py:72
  110.8 1.8 copy.57
  114.5 16.8 %all_gather.19 = bf16[1024,1,256]{0,2,1:T(8,128)(2,1)} all-gather(bf16[128,1,256]{0,2,1:T(8,128)(2,1)S(1)} %get-tuple-element.23), channel_id=1, replica_groups=mesh['grp'=4,'tok'=8,'mdl'=8] {'mdl'}, dimensions={0}, use_global_device_ids=true | all-gather | bytes 589824 | tf_op jit(solution)/shard_map/all_gather | solution.py:97
  133.1 12.9 %fusion = (f32[128,5]{0,1:T(8,128)S(1)}, f32[128,5,8192]{2,0,1:T(8,128)}) fusion(pred[128,8192]{1,0:T(8,128)(4,1)} %broadcast_compare_fusion, bf16[8192,1,256]{2,0,1:T(8,128)(2,1)} %bitcast.150, bf16[128,5,64]{2,0,1:T(8,128)(2,1)} %get-tuple-element.17, bf16[128,5,64]{2,0,1:T(8,128)(2,1)} %get-tuple-element.16), kind=kOutput, calls=%fused_computation.2 | convolution fusion | flops 1358232960 | bytes 24447488 | tf_op jit(solution)/shard_map/rcgd,kcd->rcgk/dot_general | solution.py:129
  146.1 2.2 fusion.10
  148.3 14.2 %fusion.21 = f32[1,128,128,5]{2,1,3,0:T(8,128)} fusion(bf16[8192,1,256]{2,0,1:T(8,128)(2,1)} %bitcast.151, f32[128,5,8192]{2,0,1:T(8,128)} %get-tuple-element.33, f32[128,5]{0,1:T(8,128)S(1)} %max.19, pred[128,8192]{1,0:T(8,128)(4,1)} %broadcast_compare_fusion), kind=kOutput, calls=%fused_computation.28 | convolution fusion | flops 1368391680 | bytes 24447488 | tf_op jit(solution)/shard_map/rcgk,kcd->rcgd/dot_general | solution.py:139
  162.5 10.7 %fusion.1 = f32[128,5]{0,1:T(8,128)S(1)} fusion(f32[128,5,8192]{2,0,1:T(8,128)} %get-tuple-element.33, f32[128,5]{0,1:T(8,128)S(1)} %max.19, pred[128,8192]{1,0:T(8,128)(4,1)} %broadcast_compare_fusion), kind=kLoop, calls=%fused_computation.3 | loop fusion | flops 26213760 | bytes 22025216 | tf_op jit(solution)/shard_map/reduce_sum | solution.py:138
  175.9 27.0 %all-gather.10.cloned.1.call-done = bf16[1024,640]{0,1:T(8,128)(2,1)} async-done(((bf16[128,640]{0,1:T(8,128)(2,1)}), bf16[1024,640]{0,1:T(8,128)(2,1)}) %all-gather.10.cloned.1.call-update) | async-done | bytes 1310736 | tf_op jit(solution)/shard_map/all_gather | solution.py:151
  202.9 4.0 convolution_convert_fusion.2
  206.9 36.2 %reduce-scatter.7.cloned.1.call-done = bf16[128,640]{1,0:T(8,128)(2,1)} async-done(((bf16[1024,640]{1,0:T(8,128)(2,1)}), bf16[128,640]{1,0:T(8,128)(2,1)}) %reduce-scatter.7.cloned.1.call-update) | async-done | bytes 163856 | tf_op jit(solution)/shard_map/reduce_scatter | solution.py:155
  244.2 16.7 %psum.29 = f32[128]{0:T(128)S(1)} all-reduce(f32[128]{0:T(128)S(1)} %multiply_reduce_fusion.2), channel_id=1, replica_groups=mesh['grp'=4,'tok'=8,'mdl'=8] {'mdl'}, use_global_device_ids=true, to_apply=%region_14.15 | all-reduce | flops 128 | bytes 1024 | tf_op jit(solution)/shard_map/psum | solution.py:158
  262.7 30.4 %all-gather.12.cloned.1.call-done = bf16[1024,640]{1,0:T(8,128)(2,1)} async-done(((bf16[128,640]{1,0:T(8,128)(2,1)}), bf16[1024,640]{1,0:T(8,128)(2,1)}) %all-gather.12.cloned.1.call-update) | async-done | bytes 1310736 | tf_op jit(solution)/shard_map/all_gather | solution.py:165
  293.1 10.5 %convolution_convert_fusion = bf16[1024,3584]{1,0:T(8,128)(2,1)} fusion(bf16[1024,640]{1,0:T(8,128)(2,1)} %all-gather.12.cloned.1.call-done, bf16[640,1792]{1,0:T(8,128)(2,1)} %param.28, bf16[640,1792]{1,0:T(8,128)(2,1)} %param.27), kind=kOutput, calls=%fused_computation.8 | convolution fusion | flops 4710465536 | bytes 13238272 | tf_op jit(solution)/shard_map/dot_general | solution.py:164
  303.6 53.3 %reduce-scatter.9.cloned.1.call-done = bf16[128,3584]{1,0:T(8,128)(2,1)} async-done(((bf16[1024,3584]{1,0:T(8,128)(2,1)}), bf16[128,3584]{1,0:T(8,128)(2,1)}) %reduce-scatter.9.cloned.1.call-update) | async-done | bytes 917520 | tf_op jit(solution)/shard_map/reduce_scatter | solution.py:169
  359.4 33.1 %all-gather.14.cloned.1.call-done = bf16[1024,1792]{1,0:T(8,128)(2,1)} async-done(((bf16[128,1792]{1,0:T(8,128)(2,1)}), bf16[1024,1792]{1,0:T(8,128)(2,1)}) %all-gather.14.cloned.1.call-update) | async-done | bytes 3670032 | tf_op jit(solution)/shard_map/all_gather | solution.py:174
  392.5 6.8 convolution_convert_fusion.1
  399.5 35.1 %reduce-scatter.11.cloned.1.call-done = bf16[128,640]{1,0:T(8,128)(2,1)} async-done(((bf16[1024,640]{1,0:T(8,128)(2,1)}), bf16[128,640]{1,0:T(8,128)(2,1)}) %reduce-scatter.11.cloned.1.call-update) | async-done | bytes 163856 | tf_op jit(solution)/shard_map/reduce_scatter | solution.py:178
  437.2 128.3 %psum.30 = f32[4]{0:T(128)S(1)} all-reduce(f32[4]{0:T(128)S(1)} %select_reduce_fusion.2), channel_id=1, replica_groups=mesh['grp'=4,'tok'=8,'mdl'=8] {'tok','mdl'}, use_global_device_ids=true, to_apply=%region_19.20 | all-reduce | flops 4 | bytes 32 | tf_op jit(solution)/shard_map/psum | solution.py:195
  569.9 243.1 %all-reduce.2.cloned.1.call-done = f32[16,5120]{1,0:T(8,128)} async-done(((f32[16,5120]{1,0:T(8,128)}), f32[16,5120]{1,0:T(8,128)}) %all-reduce.2.cloned.1.call-update) | async-done | bytes 327696 | tf_op jit(solution)/shard_map/psum | solution.py:196
  814.1 2.6 fusion.72
  817.4 74.3 %pmax.7 = f32[4,4]{1,0:T(4,128)} all-reduce(f32[4,4]{1,0:T(4,128)S(1)} %reshape.445), channel_id=1, replica_groups=mesh['grp'=4,'tok'=8,'mdl'=8] {'grp','tok','mdl'}, use_global_device_ids=true, to_apply=%region_24.25 | all-reduce | flops 16 | bytes 128 | tf_op jit(solution)/shard_map/pmax | solution.py:204
  (99 shorter events, 33.3 us)
Async XLA Ops:
  8.0 806.1 %copy-start = (bf16[300,5120]{1,0:T(8,128)(2,1)S(1)}, bf16[300,5120]{1,0:T(8,128)(2,1)}, u32[]{:S(2)}) copy-start(bf16[300,5120]{1,0:T(8,128)(2,1)} %param.31) | copy-start | bytes 9216004
  8.0 53.1 %all-gather.6.cloned.1.call-start = ((), (), s32[]{:S(2)}) async-start(), calls=%async_computation.4 | async-start | bytes 1474560 | tf_op jit(solution)/shard_map/all_gather | solution.py:68
  25.9 82.0 %reduce-scatter.5.cloned.1.call-start = ((), (), s32[]{:S(2)}) async-start(), calls=%async_computation.5 | async-start | bytes 4128768 | tf_op jit(solution)/shard_map/reduce_scatter | solution.py:72
  66.2 0.7 copy-start.12
  66.3 66.8 %all-gather.8.cloned.1.call-start = ((), (), s32[]{:S(2)}) async-start(), calls=%async_computation.6 | async-start | bytes 4325376 | tf_op jit(solution)/shard_map/all_gather | solution.py:123
  66.8 136.1 %all-gather.10.cloned.1.call-start = ((), (), s32[]{:S(2)}) async-start(), calls=%async_computation.7 | async-start | bytes 1474560 | tf_op jit(solution)/shard_map/all_gather | solution.py:151
  133.1 13.0 %copy-start.5 = (bf16[1024,1,256]{0,2,1:T(8,128)(2,1)S(1)}, bf16[1024,1,256]{0,2,1:T(8,128)(2,1)}, u32[]{:S(2)}) copy-start(bf16[1024,1,256]{0,2,1:T(8,128)(2,1)} %all_gather.19) | copy-start | bytes 1572868
  133.1 13.0 %copy-start.7 = (pred[128,1024]{0,1:T(8,128)(4,1)S(1)}, pred[128,1024]{0,1:T(8,128)(4,1)}, u32[]{:S(2)}) copy-start(pred[128,1024]{0,1:T(8,128)(4,1)} %fusion.43) | copy-start | bytes 393220
  133.1 13.0 %copy-start.8 = (bf16[128,5,64]{2,0,1:T(8,128)(2,1)S(1)}, bf16[128,5,64]{2,0,1:T(8,128)(2,1)}, u32[]{:S(2)}) copy-start(bf16[128,5,64]{2,0,1:T(8,128)(2,1)} %get-tuple-element.16) | copy-start | bytes 245764
  133.1 13.0 %copy-start.9 = (bf16[128,5,64]{2,0,1:T(8,128)(2,1)S(1)}, bf16[128,5,64]{2,0,1:T(8,128)(2,1)}, u32[]{:S(2)}) copy-start(bf16[128,5,64]{2,0,1:T(8,128)(2,1)} %get-tuple-element.17) | copy-start | bytes 245764
  162.5 10.7 %copy-start.1 = (f32[1024,128,5]{1,0,2:T(8,128)S(1)}, f32[1024,128,5]{1,0,2:T(8,128)}, u32[]{:S(2)}) copy-start(f32[1024,128,5]{1,0,2:T(8,128)} %get-tuple-element.31) | copy-start | bytes 7864324
  173.2 1.0 copy-start.6
  173.2 1.1 copy-start.13
  175.8 67.4 %copy-start.2 = (bf16[1,128,640]{2,1,0:T(8,128)(2,1)S(1)}, bf16[1,128,640]{2,1,0:T(8,128)(2,1)}, u32[]{:S(2)}) copy-start(bf16[1,128,640]{2,1,0:T(8,128)(2,1)} %param.16) | copy-start | bytes 491524
  175.8 85.1 %copy-start.11 = (f32[640]{0:T(1024)S(1)}, f32[640]{0:T(1024)}, u32[]{:S(2)}) copy-start(f32[640]{0:T(1024)} %param.26) | copy-start | bytes 7684
  175.8 67.4 %reduce-scatter.7.cloned.1.call-start = ((), (), s32[]{:S(2)}) async-start(), calls=%async_computation.8 | async-start | bytes 1474560 | tf_op jit(solution)/shard_map/reduce_scatter | solution.py:155
  206.9 86.2 %all-gather.12.cloned.1.call-start = ((), (), s32[]{:S(2)}) async-start(), calls=%async_computation.9 | async-start | bytes 1474560 | tf_op jit(solution)/shard_map/all_gather | solution.py:165
  262.7 94.2 %reduce-scatter.9.cloned.1.call-start = ((), (), s32[]{:S(2)}) async-start(), calls=%async_computation.10 | async-start | bytes 8257536 | tf_op jit(solution)/shard_map/reduce_scatter | solution.py:169
  303.6 88.9 %all-gather.14.cloned.1.call-start = ((), (), s32[]{:S(2)}) async-start(), calls=%async_computation.11 | async-start | bytes 4128768 | tf_op jit(solution)/shard_map/all_gather | solution.py:174
  359.3 75.3 %copy-start.3 = (bf16[128,640]{1,0:T(8,128)(2,1)S(1)}, bf16[128,640]{1,0:T(8,128)(2,1)}, u32[]{:S(2)}) copy-start(bf16[128,640]{1,0:T(8,128)(2,1)} %reduce-scatter.7.cloned.1.call-done) | copy-start | bytes 491524
  359.3 75.3 %reduce-scatter.11.cloned.1.call-start = ((), (), s32[]{:S(2)}) async-start(), calls=%async_computation.12 | async-start | bytes 1474560 | tf_op jit(solution)/shard_map/reduce_scatter | solution.py:178
  399.3 414.8 %copy-start.10 = (f32[5120]{0:T(1024)S(1)}, f32[5120]{0:T(1024)}, u32[]{:S(2)}) copy-start(f32[5120]{0:T(1024)} %param.30) | copy-start | bytes 61444
  399.4 413.6 %all-reduce.2.cloned.1.call-start = ((), (), s32[]{:S(2)}) async-start(), calls=%async_computation.13 | async-start | bytes 655360 | tf_op jit(solution)/shard_map/psum | solution.py:196
  567.5 0.7 copy-start.4
Sparse Core Ops, SparseCore 0:
  26.1 35.0 all-gather.5
  66.4 41.5 reduce-scatter.4
  175.9 26.9 all-gather.9
  207.0 36.1 reduce-scatter.6
  262.8 30.2 all-gather.11
  303.7 53.1 reduce-scatter.8
  359.4 33.0 all-gather.13
  399.5 35.0 reduce-scatter.10
Sparse Core Ops, SparseCore 1:
  69.3 56.2 all-gather.7
  568.3 244.6 all-reduce.1
where the time goes:
time: 900 us; the launch traced here: 899 us
  waiting for transfers between devices  529 us (59%)
  blocking collectives  251 us (28%)
  matrix products  59.8 us (7%)
  other arithmetic  31.8 us (4%)
  between operations  15.8 us (2%)
  local copies, waits for them, and re-layouts  11.5 us (1%)
    psum x1, waiting for transfers between devices, on_device(): last_all = lax.psum(padded, ('grp', 'tok', 'mdl'))  243 us
    psum x1, blocking collectives, on_device(): req_total = lax.psum(req_squares, ('tok', 'mdl'))  128 us
    pmax x1, blocking collectives, on_device(): lax.pmax(jnp.max(logits, -1), ('grp', 'tok', 'mdl'))  74.3 us
    reduce_scatter x1, waiting for transfers between devices, on_device(): lax.psum_scatter(partial_ffn.astype(jnp.bfloat16), 'mdl', scatter_dimensi...  53.3 us
    reduce_scatter x1, waiting for transfers between devices, on_device(): lax.psum_scatter(partial_out.astype(jnp.bfloat16), 'tok', scatter_dimensi...  36.2 us
    all_gather x1, waiting for transfers between devices, on_device(): lax.all_gather(normed, 'tok', axis=0, tiled=True)  35.1 us
    reduce_scatter x1, waiting for transfers between devices, on_device(): lax.psum_scatter(partial_down.astype(jnp.bfloat16), 'tok', scatter_dimens...  35.1 us
    reduce_scatter x1, waiting for transfers between devices, on_device(): lax.psum_scatter(partial_qkv, 'mdl', scatter_dimension=0, tiled=True)  34.7 us
  transfers between devices with their start and end apart: 10, of which 9 were waited for; matrix products, arithmetic and copies ran while one was open for 2% of the time, Pallas kernels for 0%

commit v1 on v0

--- a/solution.py
+++ b/solution.py
@@ -148,7 +148,9 @@
         .reshape(rows_mdl, heads_dev * head_dim)
     )
     partial_out = jnp.dot(
-        lax.all_gather(attended, "mdl", axis=0, tiled=True),
+        jnp.concatenate(
+            lax.all_to_all(jnp.stack([attended] * lax.axis_size("mdl")), "mdl", 0, 0), axis=0
+        ),
         w_out,
         preferred_element_type=jnp.float32,
     )

time: 900 us -> 892 us (level)
  waiting for transfers between devices: 529 us -> 501 us
  blocking collectives: 251 us -> 273 us
    all_gather x1 -> x0, waiting for transfers between devices: 27 us -> none  [on_device(): lax.all_gather(attended, 'mdl', axis=0, tiled=True)]
    all_to_all x0 -> x1, blocking collectives: none -> 21.6 us  [on_device(): lax.all_to_all(jnp.stack([attended] * lax.axis_size('mdl')), 'mdl', 0, 0)]
  transfers between devices with their start and end apart: 10 -> 9, of which waited for: 9 -> 8; matrix products, arithmetic and copies ran while one was open for 2% -> 2% of each run, Pallas kernels for 0% -> 0%
where the time goes in v1:
time: 892 us; the launch traced here: 891 us
  waiting for transfers between devices  501 us (56%)
  blocking collectives  273 us (31%)
  matrix products  57.5 us (6%)
  other arithmetic  31.8 us (4%)
  between operations  15.8 us (2%)
  local copies, waits for them, and re-layouts  11.8 us (1%)
    psum x1, waiting for transfers between devices, on_device(): last_all = lax.psum(padded, ('grp', 'tok', 'mdl'))  243 us
    psum x1, blocking collectives, on_device(): req_total = lax.psum(req_squares, ('tok', 'mdl'))  128 us
    pmax x1, blocking collectives, on_device(): lax.pmax(jnp.max(logits, -1), ('grp', 'tok', 'mdl'))  74.3 us
    reduce_scatter x1, waiting for transfers between devices, on_device(): lax.psum_scatter(partial_ffn.astype(jnp.bfloat16), 'mdl', scatter_dimensi...  53.3 us
    all_gather x1, waiting for transfers between devices, on_device(): lax.all_gather(normed, 'tok', axis=0, tiled=True)  35.1 us
    reduce_scatter x1, waiting for transfers between devices, on_device(): lax.psum_scatter(partial_out.astype(jnp.bfloat16), 'tok', scatter_dimensi...  35.1 us
    reduce_scatter x1, waiting for transfers between devices, on_device(): lax.psum_scatter(partial_down.astype(jnp.bfloat16), 'tok', scatter_dimens...  35.1 us
    reduce_scatter x1, waiting for transfers between devices, on_device(): lax.psum_scatter(partial_qkv, 'mdl', scatter_dimension=0, tiled=True)  34.7 us
  transfers between devices with their start and end apart: 9, of which 8 were waited for; matrix products, arithmetic and copies ran while one was open for 2% of the time, Pallas kernels for 0%

profile of v1, /device:TPU:1, one launch (start us, length us, event | category | flops | bytes accessed | tf_op | source)
XLA Modules:
  0.0 890.6 jit_solution(14090036110246574709)
XLA Ops:
  9.2 15.0 %psum.28 = f32[128]{0:T(128)S(1)} all-reduce(f32[128]{0:T(128)S(1)} %fusion.44), channel_id=1, replica_groups=mesh['grp'=4,'tok'=8,'mdl'=8] {'mdl'}, use_global_device_ids=true, to_apply=%region_1.0 | all-reduce | flops 128 | bytes 1024 | tf_op jit(solution)/shard_map/psum | solution.py:62
  26.0 35.1 %all-gather.5.cloned.1.call-done = bf16[1024,640]{1,0:T(8,128)(2,1)} async-done(((bf16[128,640]{1,0:T(8,128)(2,1)}), bf16[1024,640]{1,0:T(8,128)(2,1)}) %all-gather.5.cloned.1.call-update) | async-done | bytes 1310736 | tf_op jit(solution)/shard_map/all_gather | solution.py:68
  61.1 5.1 fusion.30
  73.3 34.7 %reduce-scatter.5.cloned.1.call-done = f32[128,896]{0,1:T(8,128)} async-done(((f32[1024,896]{0,1:T(8,128)}), f32[128,896]{0,1:T(8,128)}) %reduce-scatter.5.cloned.1.call-update) | async-done | bytes 458768 | tf_op jit(solution)/shard_map/reduce_scatter | solution.py:72
  110.8 1.8 copy.62
  114.5 16.8 %all_gather.16 = bf16[1024,1,256]{0,2,1:T(8,128)(2,1)} all-gather(bf16[128,1,256]{0,2,1:T(8,128)(2,1)S(1)} %get-tuple-element.23), channel_id=1, replica_groups=mesh['grp'=4,'tok'=8,'mdl'=8] {'mdl'}, dimensions={0}, use_global_device_ids=true | all-gather | bytes 589824 | tf_op jit(solution)/shard_map/all_gather | solution.py:97
  133.1 12.9 %fusion = (f32[128,5]{0,1:T(8,128)S(1)}, f32[128,5,8192]{2,0,1:T(8,128)}) fusion(pred[128,8192]{1,0:T(8,128)(4,1)} %broadcast_compare_fusion, bf16[8192,1,256]{2,0,1:T(8,128)(2,1)} %bitcast.152, bf16[128,5,64]{2,0,1:T(8,128)(2,1)} %get-tuple-element.17, bf16[128,5,64]{2,0,1:T(8,128)(2,1)} %get-tuple-element.16), kind=kOutput, calls=%fused_computation.2 | convolution fusion | flops 1358232960 | bytes 24447488 | tf_op jit(solution)/shard_map/rcgd,kcd->rcgk/dot_general | solution.py:129
  146.1 2.2 fusion.10
  148.3 14.2 %fusion.21 = f32[1,128,128,5]{2,1,3,0:T(8,128)} fusion(bf16[8192,1,256]{2,0,1:T(8,128)(2,1)} %bitcast.153, f32[128,5,8192]{2,0,1:T(8,128)} %get-tuple-element.33, f32[128,5]{0,1:T(8,128)S(1)} %max.19, pred[128,8192]{1,0:T(8,128)(4,1)} %broadcast_compare_fusion), kind=kOutput, calls=%fused_computation.28 | convolution fusion | flops 1368391680 | bytes 24447488 | tf_op jit(solution)/shard_map/rcgk,kcd->rcgd/dot_general | solution.py:139
  162.5 10.7 %fusion.1 = f32[128,5]{0,1:T(8,128)S(1)} fusion(f32[128,5,8192]{2,0,1:T(8,128)} %get-tuple-element.33, f32[128,5]{0,1:T(8,128)S(1)} %max.19, pred[128,8192]{1,0:T(8,128)(4,1)} %broadcast_compare_fusion), kind=kLoop, calls=%fused_computation.3 | loop fusion | flops 26213760 | bytes 22025216 | tf_op jit(solution)/shard_map/reduce_sum | solution.py:138
  175.4 21.6 %all_to_all.5 = bf16[8,128,640]{2,1,0:T(8,128)(2,1)S(1)} all-to-all(bf16[8,128,640]{2,1,0:T(8,128)(2,1)S(1)} %stack.3), channel_id=1, replica_groups=mesh['grp'=4,'tok'=8,'mdl'=8] {'mdl'}, dimensions={0} | all-to-all | bytes 2621440 | tf_op jit(solution)/shard_map/all_to_all | solution.py:152
  197.0 2.4 convolution_convert_fusion.2
  199.5 35.1 %reduce-scatter.7.cloned.1.call-done = bf16[128,640]{1,0:T(8,128)(2,1)} async-done(((bf16[1024,640]{1,0:T(8,128)(2,1)}), bf16[128,640]{1,0:T(8,128)(2,1)}) %reduce-scatter.7.cloned.1.call-update) | async-done | bytes 163856 | tf_op jit(solution)/shard_map/reduce_scatter | solution.py:157
  235.7 16.7 %psum.29 = f32[128]{0:T(128)S(1)} all-reduce(f32[128]{0:T(128)S(1)} %multiply_reduce_fusion.2), channel_id=1, replica_groups=mesh['grp'=4,'tok'=8,'mdl'=8] {'mdl'}, use_global_device_ids=true, to_apply=%region_14.15 | all-reduce | flops 128 | bytes 1024 | tf_op jit(solution)/shard_map/psum | solution.py:160
  254.2 30.4 %all-gather.9.cloned.1.call-done = bf16[1024,640]{1,0:T(8,128)(2,1)} async-done(((bf16[128,640]{1,0:T(8,128)(2,1)}), bf16[1024,640]{1,0:T(8,128)(2,1)}) %all-gather.9.cloned.1.call-update) | async-done | bytes 1310736 | tf_op jit(solution)/shard_map/all_gather | solution.py:167
  284.6 10.5 %convolution_convert_fusion = bf16[1024,3584]{1,0:T(8,128)(2,1)} fusion(bf16[1024,640]{1,0:T(8,128)(2,1)} %all-gather.9.cloned.1.call-done, bf16[640,1792]{1,0:T(8,128)(2,1)} %param.28, bf16[640,1792]{1,0:T(8,128)(2,1)} %param.27), kind=kOutput, calls=%fused_computation.8 | convolution fusion | flops 4710465536 | bytes 13238272 | tf_op jit(solution)/shard_map/dot_general | solution.py:166
  295.1 53.3 %reduce-scatter.9.cloned.1.call-done = bf16[128,3584]{1,0:T(8,128)(2,1)} async-done(((bf16[1024,3584]{1,0:T(8,128)(2,1)}), bf16[128,3584]{1,0:T(8,128)(2,1)}) %reduce-scatter.9.cloned.1.call-update) | async-done | bytes 917520 | tf_op jit(solution)/shard_map/reduce_scatter | solution.py:171
  350.9 33.1 %all-gather.11.cloned.1.call-done = bf16[1024,1792]{1,0:T(8,128)(2,1)} async-done(((bf16[128,1792]{1,0:T(8,128)(2,1)}), bf16[1024,1792]{1,0:T(8,128)(2,1)}) %all-gather.11.cloned.1.call-update) | async-done | bytes 3670032 | tf_op jit(solution)/shard_map/all_gather | solution.py:176
  384.0 6.8 convolution_convert_fusion.1
  391.0 35.1 %reduce-scatter.11.cloned.1.call-done = bf16[128,640]{1,0:T(8,128)(2,1)} async-done(((bf16[1024,640]{1,0:T(8,128)(2,1)}), bf16[128,640]{1,0:T(8,128)(2,1)}) %reduce-scatter.11.cloned.1.call-update) | async-done | bytes 163856 | tf_op jit(solution)/shard_map/reduce_scatter | solution.py:180
  428.7 128.3 %psum.30 = f32[4]{0:T(128)S(1)} all-reduce(f32[4]{0:T(128)S(1)} %select_reduce_fusion.2), channel_id=1, replica_groups=mesh['grp'=4,'tok'=8,'mdl'=8] {'tok','mdl'}, use_global_device_ids=true, to_apply=%region_19.20 | all-reduce | flops 4 | bytes 32 | tf_op jit(solution)/shard_map/psum | solution.py:197
  561.4 243.1 %all-reduce.2.cloned.1.call-done = f32[16,5120]{1,0:T(8,128)} async-done(((f32[16,5120]{1,0:T(8,128)}), f32[16,5120]{1,0:T(8,128)}) %all-reduce.2.cloned.1.call-update) | async-done | bytes 327696 | tf_op jit(solution)/shard_map/psum | solution.py:198
  805.7 2.6 fusion.72
  808.9 74.3 %pmax.7 = f32[4,4]{1,0:T(4,128)} all-reduce(f32[4,4]{1,0:T(4,128)S(1)} %reshape.447), channel_id=1, replica_groups=mesh['grp'=4,'tok'=8,'mdl'=8] {'grp','tok','mdl'}, use_global_device_ids=true, to_apply=%region_24.25 | all-reduce | flops 16 | bytes 128 | tf_op jit(solution)/shard_map/pmax | solution.py:206
  (101 shorter events, 32.8 us)
Async XLA Ops:
  8.0 797.7 %copy-start = (bf16[300,5120]{1,0:T(8,128)(2,1)S(1)}, bf16[300,5120]{1,0:T(8,128)(2,1)}, u32[]{:S(2)}) copy-start(bf16[300,5120]{1,0:T(8,128)(2,1)} %param.31) | copy-start | bytes 9216004
  8.0 53.1 %all-gather.5.cloned.1.call-start = ((), (), s32[]{:S(2)}) async-start(), calls=%async_computation.5 | async-start | bytes 1474560 | tf_op jit(solution)/shard_map/all_gather | solution.py:68
  25.9 82.0 %reduce-scatter.5.cloned.1.call-start = ((), (), s32[]{:S(2)}) async-start(), calls=%async_computation.6 | async-start | bytes 4128768 | tf_op jit(solution)/shard_map/reduce_scatter | solution.py:72
  66.2 0.7 copy-start.13
  66.3 66.8 %all-gather.7.cloned.1.call-start = ((), (), s32[]{:S(2)}) async-start(), calls=%async_computation.7 | async-start | bytes 4325376 | tf_op jit(solution)/shard_map/all_gather | solution.py:123
  66.8 167.8 %reduce-scatter.7.cloned.1.call-start = ((), (), s32[]{:S(2)}) async-start(), calls=%async_computation.8 | async-start | bytes 1474560 | tf_op jit(solution)/shard_map/reduce_scatter | solution.py:157
  133.1 13.0 %copy-start.5 = (bf16[1024,1,256]{0,2,1:T(8,128)(2,1)S(1)}, bf16[1024,1,256]{0,2,1:T(8,128)(2,1)}, u32[]{:S(2)}) copy-start(bf16[1024,1,256]{0,2,1:T(8,128)(2,1)} %all_gather.16) | copy-start | bytes 1572868
  133.1 13.0 %copy-start.7 = (pred[128,1024]{0,1:T(8,128)(4,1)S(1)}, pred[128,1024]{0,1:T(8,128)(4,1)}, u32[]{:S(2)}) copy-start(pred[128,1024]{0,1:T(8,128)(4,1)} %fusion.43) | copy-start | bytes 393220
  133.1 13.0 %copy-start.8 = (bf16[128,5,64]{2,0,1:T(8,128)(2,1)S(1)}, bf16[128,5,64]{2,0,1:T(8,128)(2,1)}, u32[]{:S(2)}) copy-start(bf16[128,5,64]{2,0,1:T(8,128)(2,1)} %get-tuple-element.16) | copy-start | bytes 245764
  133.1 13.0 %copy-start.9 = (bf16[128,5,64]{2,0,1:T(8,128)(2,1)S(1)}, bf16[128,5,64]{2,0,1:T(8,128)(2,1)}, u32[]{:S(2)}) copy-start(bf16[128,5,64]{2,0,1:T(8,128)(2,1)} %get-tuple-element.17) | copy-start | bytes 245764
  162.5 10.7 %copy-start.1 = (f32[1024,128,5]{1,0,2:T(8,128)S(1)}, f32[1024,128,5]{1,0,2:T(8,128)}, u32[]{:S(2)}) copy-start(f32[1024,128,5]{1,0,2:T(8,128)} %get-tuple-element.31) | copy-start | bytes 7864324
  173.2 1.0 copy-start.6
  173.2 1.1 copy-start.14
  175.3 21.8 %copy-start.12 = (bf16[640,640]{1,0:T(8,128)(2,1)S(1)}, bf16[640,640]{1,0:T(8,128)(2,1)}, u32[]{:S(2)}) copy-start(bf16[640,640]{1,0:T(8,128)(2,1)} %param.25) | copy-start | bytes 2457604
  197.0 37.6 %copy-start.2 = (bf16[1,128,640]{2,1,0:T(8,128)(2,1)S(1)}, bf16[1,128,640]{2,1,0:T(8,128)(2,1)}, u32[]{:S(2)}) copy-start(bf16[1,128,640]{2,1,0:T(8,128)(2,1)} %param.16) | copy-start | bytes 491524
  197.0 55.4 %copy-start.11 = (f32[640]{0:T(1024)S(1)}, f32[640]{0:T(1024)}, u32[]{:S(2)}) copy-start(f32[640]{0:T(1024)} %param.26) | copy-start | bytes 7684
  199.4 85.2 %all-gather.9.cloned.1.call-start = ((), (), s32[]{:S(2)}) async-start(), calls=%async_computation.9 | async-start | bytes 1474560 | tf_op jit(solution)/shard_map/all_gather | solution.py:167
  254.1 94.3 %reduce-scatter.9.cloned.1.call-start = ((), (), s32[]{:S(2)}) async-start(), calls=%async_computation.10 | async-start | bytes 8257536 | tf_op jit(solution)/shard_map/reduce_scatter | solution.py:171
  295.1 88.9 %all-gather.11.cloned.1.call-start = ((), (), s32[]{:S(2)}) async-start(), calls=%async_computation.11 | async-start | bytes 4128768 | tf_op jit(solution)/shard_map/all_gather | solution.py:176
  350.8 75.3 %copy-start.3 = (bf16[128,640]{1,0:T(8,128)(2,1)S(1)}, bf16[128,640]{1,0:T(8,128)(2,1)}, u32[]{:S(2)}) copy-start(bf16[128,640]{1,0:T(8,128)(2,1)} %reduce-scatter.7.cloned.1.call-done) | copy-start | bytes 491524
  350.8 75.3 %reduce-scatter.11.cloned.1.call-start = ((), (), s32[]{:S(2)}) async-start(), calls=%async_computation.12 | async-start | bytes 1474560 | tf_op jit(solution)/shard_map/reduce_scatter | solution.py:180
  390.8 414.8 %copy-start.10 = (f32[5120]{0:T(1024)S(1)}, f32[5120]{0:T(1024)}, u32[]{:S(2)}) copy-start(f32[5120]{0:T(1024)} %param.30) | copy-start | bytes 61444
  390.9 413.6 %all-reduce.2.cloned.1.call-start = ((), (), s32[]{:S(2)}) async-start(), calls=%async_computation.13 | async-start | bytes 655360 | tf_op jit(solution)/shard_map/psum | solution.py:198
  559.0 0.7 copy-start.4
Sparse Core Ops, SparseCore 0:
  26.1 35.0 all-gather.4
  66.4 41.5 reduce-scatter.4
  199.6 35.0 reduce-scatter.6
  254.2 30.3 all-gather.8
  295.2 53.1 reduce-scatter.8
  350.9 33.0 all-gather.10
  391.0 35.0 reduce-scatter.10
Sparse Core Ops, SparseCore 1:
  69.3 56.2 all-gather.6
  559.8 244.7 all-reduce.1
